TPU v7x, 256 devices: a whole 4x4x8 slice. The times are simulated.
256 devices in a mesh: dp: 32 (over z, x), et: 8 (over y, core).
Axes of the slice: x: 4, y: 4, z: 8, core: 2. Of those that a mesh axis runs over, the one named last changes fastest.
Arguments:
- tokens: bfloat16 [4096, 2048], P('dp', 'et'), may hold values from -6 to 6
- cotangent: bfloat16 [4096, 2048], P('dp', 'et'), may hold values from -1.5 to 1.5
- expert_ids: int32 [4096, 8], P('dp'), may hold values from 0 to 63, all different within a row; in each aligned block of 128 rows (0 to 127, 128 to 255, ...) at most 24 rows name the same one
- route_gates: bfloat16 [4096, 8], P('dp'), may hold values from 0.049804688 to 0.3984375
- gate_proj: bfloat16 [64, 2048, 1024], P('dp', None, 'et'), may hold values from -0.125 to 0.125
- up_proj: bfloat16 [64, 2048, 1024], P('dp', None, 'et'), may hold values from -0.125 to 0.125
- down_proj: bfloat16 [64, 1024, 2048], P('dp', 'et'), may hold values from -0.1875 to 0.1875
Outputs:
- mixed: bfloat16 [4096, 2048], P('dp', 'et')
- grad_tokens: bfloat16 [4096, 2048], P('dp', 'et')
- grad_gates: float32 [4096, 8], P('dp')
- grad_gate_proj: float32 [64, 2048, 1024], P('dp', None, 'et')
- grad_up_proj: float32 [64, 2048, 1024], P('dp', None, 'et')
- grad_down_proj: float32 [64, 1024, 2048], P('dp', 'et')
Inputs may be any that keep to these rules, and one draw needn't show every extreme that they name: `expert_ids`: each row names 8 different experts. Among the rows of one device (128 aligned rows), no expert is named more than 24 times, a bound that some block reaches.
All inputs are finite; a program needn't handle non-finite values.
Results may differ from a plain program's by a relative error of at most 0.015.
Values may be sent and summed in bfloat16 or wider, within the bound.
No kernel may reach another device: no remote copies, remote signals or barrier semaphores. Data moves between devices by JAX's collectives and lax.ppermute only.
A program may use at most 128 MiB of HBM per device.

v0:
```python
import jax
import jax.numpy as jnp
from jax import lax
from jax.sharding import PartitionSpec as P


def places_in_block(chosen, experts):
    flattened = chosen.reshape(-1)
    pairs = flattened.shape[0]
    onehot = (flattened[:, None] == jnp.arange(experts, dtype=jnp.int32)[None, :]).astype(
        jnp.bfloat16
    )
    rows = lax.broadcasted_iota(jnp.int32, (pairs, pairs), 0)
    cols = lax.broadcasted_iota(jnp.int32, (pairs, pairs), 1)
    earlier = (cols < rows).astype(jnp.bfloat16)
    before = jnp.dot(earlier, onehot, preferred_element_type=jnp.float32)
    return jnp.sum(before * onehot.astype(jnp.float32), axis=1).astype(jnp.int32)


def local(tokens, cotangent, expert_ids, route_gates, gate_proj, up_proj, down_proj):
    groups = lax.axis_size("dp")
    shards = lax.axis_size("et")
    local_experts, features, units = gate_proj.shape
    experts = local_experts * groups
    tok_rows, per_token = expert_ids.shape
    width = tokens.shape[1]
    capacity = 3 * tok_rows * per_token // (2 * experts)
    slots = experts * capacity
    places = places_in_block(expert_ids, experts)
    slot_index = (expert_ids.reshape(-1) * capacity + places).reshape(tok_rows, per_token)
    by_pair = slot_index.T
    match = by_pair[None, :, :] == jnp.arange(slots, dtype=jnp.int32)[:, None, None]
    select = jnp.any(match, axis=1).astype(jnp.bfloat16)
    gate_select = jnp.sum(
        jnp.where(match, route_gates.T[None, :, :].astype(jnp.float32), 0.0), axis=1
    ).astype(jnp.bfloat16)
    picked = jnp.dot(select, tokens, preferred_element_type=jnp.float32).astype(jnp.bfloat16)
    scaled = jnp.dot(gate_select, cotangent, preferred_element_type=jnp.float32).astype(
        jnp.bfloat16
    )
    routed = jnp.stack([picked, scaled]).reshape(2, experts, capacity, width)
    routed = lax.all_to_all(routed, "dp", split_axis=1, concat_axis=2, tiled=True)
    gathered = lax.all_gather(routed, "et", axis=0)
    expert_in = gathered[:, 0]
    expert_cot = gathered[:, 1]
    gate_w = gate_proj.reshape(local_experts, shards, width, units)
    up_w = up_proj.reshape(local_experts, shards, width, units)
    down_w = down_proj.reshape(local_experts, units, shards, width)
    pre_gate = jnp.einsum("jesd,ejdf->esf", expert_in, gate_w, preferred_element_type=jnp.float32)
    pre_up = jnp.einsum("jesd,ejdf->esf", expert_in, up_w, preferred_element_type=jnp.float32)
    sigmoid_gate = jax.nn.sigmoid(pre_gate)
    silu_gate = pre_gate * sigmoid_gate
    hidden = (silu_gate * pre_up).astype(jnp.bfloat16)
    out_part = jnp.einsum("esf,efd->esd", hidden, down_proj, preferred_element_type=jnp.float32)
    grad_hidden = jnp.einsum(
        "jesd,efjd->esf", expert_cot, down_w, preferred_element_type=jnp.float32
    )
    grad_pre_gate = (
        grad_hidden * pre_up * sigmoid_gate * (1.0 + pre_gate * (1.0 - sigmoid_gate))
    ).astype(jnp.bfloat16)
    grad_pre_up = (grad_hidden * silu_gate).astype(jnp.bfloat16)
    grad_down = jnp.einsum(
        "esf,jesd->efjd", hidden, expert_cot, preferred_element_type=jnp.float32
    ).reshape(local_experts, units, features)
    grad_gate_w = jnp.einsum(
        "jesd,esf->ejdf", expert_in, grad_pre_gate, preferred_element_type=jnp.float32
    ).reshape(local_experts, features, units)
    grad_up_w = jnp.einsum(
        "jesd,esf->ejdf", expert_in, grad_pre_up, preferred_element_type=jnp.float32
    ).reshape(local_experts, features, units)
    in_part = jnp.einsum(
        "esf,edf->esd", grad_pre_gate, gate_proj, preferred_element_type=jnp.float32
    )
    in_part = in_part + jnp.einsum(
        "esf,edf->esd", grad_pre_up, up_proj, preferred_element_type=jnp.float32
    )
    out_sum, in_sum = (
        lax.psum_scatter(out_part.astype(jnp.bfloat16), "et", scatter_dimension=2, tiled=True),
        lax.psum_scatter(in_part.astype(jnp.bfloat16), "et", scatter_dimension=2, tiled=True),
    )
    back_out, back_grad = (
        lax.all_to_all(out_sum, "dp", split_axis=1, concat_axis=0, tiled=True),
        lax.all_to_all(in_sum, "dp", split_axis=1, concat_axis=0, tiled=True),
    )
    back_out = back_out.reshape(slots, width)
    back_grad = back_grad.reshape(slots, width)
    mixed = jnp.einsum(
        "st,sd->td", gate_select, back_out, preferred_element_type=jnp.float32
    ).astype(jnp.bfloat16)
    grad_tokens = jnp.einsum(
        "st,sd->td", select, back_grad, preferred_element_type=jnp.float32
    ).astype(jnp.bfloat16)
    out_rows = (
        back_out[slot_index.reshape(-1)].reshape(tok_rows, per_token, width).astype(jnp.float32)
    )
    gate_part = jnp.sum(cotangent.astype(jnp.float32)[:, None, :] * out_rows, axis=2)
    grad_gates = lax.psum(gate_part, "et")
    return (mixed, grad_tokens, grad_gates, grad_gate_w, grad_up_w, grad_down)


def solution(mesh):
    in_specs = (
        P("dp", "et"),
        P("dp", "et"),
        P("dp", None),
        P("dp", None),
        P("dp", None, "et"),
        P("dp", None, "et"),
        P("dp", "et", None),
    )
    out_specs = (
        P("dp", "et"),
        P("dp", "et"),
        P("dp", None),
        P("dp", None, "et"),
        P("dp", None, "et"),
        P("dp", "et", None),
    )
    return jax.shard_map(local, mesh=mesh, in_specs=in_specs, out_specs=out_specs, check_vma=False)
```

profile of v0, /device:TPU:2, one launch (start us, length us, event | category | flops | bytes accessed | tf_op | source)
XLA Modules:
  0.0 328.7 jit_solution(484087539045145669)
XLA Ops:
  9.6 5.6 %fusion = pred[1536,128]{1,0:T(8,128)(4,1)S(1)} fusion(s32[8,128]{1,0:T(8,128)S(1)} %copy.67), kind=kLoop, calls=%fused_computation.6 | loop fusion | flops 2949120 | bytes 200704 | tf_op jit(solution)/shard_map/reduce_or | solution.py:33
  15.2 8.1 %select_reduce_fusion = bf16[1536,128]{1,0:T(8,128)(2,1)S(1)} fusion(f32[8,128]{1,0:T(8,128)S(1)} %convert_bitcast_fusion, s32[8,128]{1,0:T(8,128)S(1)} %copy.67), kind=kLoop, calls=%fused_computation.4 | loop fusion | flops 4521984 | bytes 401408 | tf_op jit(solution)/shard_map/reduce_sum | solution.py:34
  24.6 1.3 convolution_convert_fusion.2
  26.1 50.7 %all_to_all.45 = bf16[2,64,24,256]{3,2,0,1:T(8,128)(2,1)S(1)} all-to-all(bf16[2,64,24,256]{3,2,0,1:T(8,128)(2,1)S(1)} %pad_maximum_fusion), channel_id=1, replica_groups=mesh['dp'=32,'et'=8] {'dp'}, dimensions={1} | all-to-all | bytes 3145728 | tf_op jit(solution)/shard_map/all_to_all | solution.py:42
  76.8 1.2 copy.70
  78.3 66.7 %all-gather.2.cloned.1.call-done = bf16[8,2,2,768,256]{4,3,0,2,1:T(8,128)(2,1)} async-done(((bf16[1,2,2,768,256]{4,3,0,2,1:T(8,128)(2,1)}), bf16[8,2,2,768,256]{4,3,0,2,1:T(8,128)(2,1)}) %all-gather.2.cloned.1.call-update) | async-done | bytes 12582928 | tf_op jit(solution)/shard_map/all_gather | solution.py:43
  145.0 4.7 %fusion.9 = f32[2,768,128]{2,1,0:T(8,128)S(1)} fusion(bf16[2,8,256,128]{3,2,1,0:T(8,128)(2,1)S(1)} %bitcast.108, bf16[8,2,2,768,256]{4,3,0,2,1:T(8,128)(2,1)} %all-gather.2.cloned.1.call-done), kind=kOutput, calls=%fused_computation.20 | convolution fusion | flops 805306368 | bytes 8126464 | tf_op jit(solution)/shard_map/jesd,ejdf->esf/dot_general | solution.py:50
  149.7 5.2 %fusion.8 = f32[2,768,128]{2,1,0:T(8,128)S(1)} fusion(bf16[2,8,256,128]{3,2,1,0:T(8,128)(2,1)S(1)} %bitcast.96, bf16[8,2,2,768,256]{4,3,0,2,1:T(8,128)(2,1)} %all-gather.2.cloned.1.call-done), kind=kOutput, calls=%fused_computation.19 | convolution fusion | flops 805306368 | bytes 8126464 | tf_op jit(solution)/shard_map/jesd,ejdf->esf/dot_general | solution.py:49
  154.9 2.0 multiply_convert_fusion
  157.7 4.4 %convolution_convert_fusion = bf16[2,768,2048]{2,1,0:T(8,128)(2,1)} fusion(bf16[2,768,128]{2,1,0:T(8,128)(2,1)S(1)} %get-tuple-element.32, bf16[2,128,2048]{2,1,0:T(8,128)(2,1)S(1)} %copy-done.10), kind=kOutput, calls=%fused_computation.9 | convolution fusion | flops 808452096 | bytes 7733248 | tf_op jit(solution)/shard_map/esf,efd->esd/dot_general | solution.py:54
  162.2 1.8 fusion.24
  164.0 4.4 %add_convert_fusion = bf16[2,768,2048]{2,1,0:T(8,128)(2,1)} fusion(f32[2,768,2048]{2,1,0:T(8,128)S(1)} %fusion.24, bf16[2,768,128]{2,1,0:T(8,128)(2,1)S(1)} %get-tuple-element.30, bf16[2,2048,128]{2,1,0:T(8,128)(2,1)S(1)} %copy-done.9), kind=kOutput, calls=%fused_computation.1 | convolution fusion | flops 811597824 | bytes 20316160 | tf_op jit(solution)/shard_map/esf,edf->esd/dot_general | solution.py:74
  168.4 39.3 %reduce-scatter.3.cloned.1.call-done = bf16[2,768,256]{2,1,0:T(8,128)(2,1)} async-done(((bf16[2,768,2048]{2,1,0:T(8,128)(2,1)}), bf16[2,768,256]{2,1,0:T(8,128)(2,1)}) %reduce-scatter.3.cloned.1.call-update) | async-done | bytes 786448 | tf_op jit(solution)/shard_map/reduce_scatter | solution.py:78
  207.7 2.8 copy.71
  210.5 10.1 %all-to-all-start.1 = ((bf16[2,768,256]{2,0,1:T(2,128)(2,1)}), bf16[2,768,256]{2,0,1:T(2,128)(2,1)S(1)}, u32[]{:S(2)}, u32[]{:S(2)}) async-start(bf16[2,768,256]{2,0,1:T(2,128)(2,1)} %copy.71), calls=%async_computation.2 | async-start | bytes 1572864 | tf_op jit(solution)/shard_map/all_to_all | solution.py:82
  221.5 33.8 %reduce-scatter.5.cloned.1.call-done = bf16[2,768,256]{2,1,0:T(8,128)(2,1)} async-done(((bf16[2,768,2048]{2,1,0:T(8,128)(2,1)}), bf16[2,768,256]{2,1,0:T(8,128)(2,1)}) %reduce-scatter.5.cloned.1.call-update) | async-done | bytes 786448 | tf_op jit(solution)/shard_map/reduce_scatter | solution.py:79
  255.3 2.9 copy.74
  258.2 10.1 %all-to-all-start.2 = ((bf16[2,768,256]{2,0,1:T(2,128)(2,1)}), bf16[2,768,256]{2,0,1:T(2,128)(2,1)}, u32[]{:S(2)}, u32[]{:S(2)}) async-start(bf16[2,768,256]{2,0,1:T(2,128)(2,1)} %copy.74), calls=%async_computation.4 | async-start | bytes 1572864 | tf_op jit(solution)/shard_map/all_to_all | solution.py:83
  268.3 5.5 %fusion.1 = f32[2,128,8,256]{1,3,2,0:T(8,128)S(1)} fusion(bf16[8,2,2,768,256]{4,3,0,2,1:T(8,128)(2,1)} %all-gather.2.cloned.1.call-done, bf16[2,768,128]{2,1,0:T(8,128)(2,1)} %copy-done.8), kind=kOutput, calls=%fused_computation.7 | convolution fusion | flops 805306368 | bytes 8781824 | tf_op jit(solution)/shard_map/esf,jesd->efjd/dot_general | solution.py:62
  273.8 1.8 copy.82
  275.6 6.7 %fusion.4 = f32[2,8,256,128]{3,2,1,0:T(8,128)} fusion(bf16[8,2,2,768,256]{4,3,0,2,1:T(8,128)(2,1)} %all-gather.2.cloned.1.call-done, bf16[2,768,128]{2,1,0:T(8,128)(2,1)} %copy-done.7), kind=kOutput, calls=%fused_computation.12 | convolution fusion | flops 805306368 | bytes 8781824 | tf_op jit(solution)/shard_map/jesd,esf->ejdf/dot_general | solution.py:68
  282.3 6.7 %fusion.5 = f32[2,8,256,128]{3,2,1,0:T(8,128)} fusion(bf16[8,2,2,768,256]{4,3,0,2,1:T(8,128)(2,1)} %all-gather.2.cloned.1.call-done, bf16[2,768,128]{2,1,0:T(8,128)(2,1)S(1)} %copy-done.6), kind=kOutput, calls=%fused_computation.13 | convolution fusion | flops 805306368 | bytes 8781824 | tf_op jit(solution)/shard_map/jesd,esf->ejdf/dot_general | solution.py:65
  289.2 3.9 %gather_fusion = bf16[1024,256]{1,0:T(8,128)(2,1)S(1)} fusion(bf16[1536,256]{1,0:T(8,128)(2,1)S(1)} %bitcast.97, s32[1024]{0:T(1024)S(1)} %broadcast_clamp_fusion), kind=kCustom, calls=%fused_computation | custom fusion | bytes 1052672 | tf_op jit(solution)/shard_map/gather | solution.py:94
  293.4 24.7 %psum.7 = f32[128,8]{1,0:T(8,128)S(1)} all-reduce(f32[128,8]{1,0:T(8,128)S(1)} %fusion.15), channel_id=1, replica_groups=mesh['dp'=32,'et'=8] {'et'}, use_global_device_ids=true, to_apply=%region_6.7 | all-reduce | flops 1024 | bytes 8192 | tf_op jit(solution)/shard_map/psum | solution.py:97
  (59 shorter events, 9.9 us)
Async XLA Ops:
  7.2 142.5 %copy-start = (bf16[2,2048,128]{2,1,0:T(8,128)(2,1)S(1)}, bf16[2,2048,128]{2,1,0:T(8,128)(2,1)}, u32[]{:S(2)}) copy-start(bf16[2,2048,128]{2,1,0:T(8,128)(2,1)} %param.11) | copy-start | bytes 3145732
  7.2 137.8 %all-gather.2.cloned.1.call-start = ((), (), s32[]{:S(2)}) async-start(), calls=%async_computation.5 | async-start | bytes 14155776 | tf_op jit(solution)/shard_map/all_gather | solution.py:43
  15.2 10.7 %copy-start.11 = (pred[1536,128]{1,0:T(8,128)(4,1)}, pred[1536,128]{1,0:T(8,128)(4,1)S(1)}, u32[]{:S(2)}) copy-start(pred[1536,128]{1,0:T(8,128)(4,1)S(1)} %fusion) | copy-start | bytes 589828
  24.6 120.4 %copy-start.9 = (bf16[2,2048,128]{2,1,0:T(8,128)(2,1)S(1)}, bf16[2,2048,128]{2,1,0:T(8,128)(2,1)}, u32[]{:S(2)}) copy-start(bf16[2,2048,128]{2,1,0:T(8,128)(2,1)} %param.12) | copy-start | bytes 3145732
  78.0 129.7 %reduce-scatter.3.cloned.1.call-start = ((), (), s32[]{:S(2)}) async-start(), calls=%async_computation.6 | async-start | bytes 7077888 | tf_op jit(solution)/shard_map/reduce_scatter | solution.py:78
  144.9 10.0 %copy-start.2 = (bf16[8,2,2,768,256]{4,3,0,2,1:T(8,128)(2,1)S(1)}, bf16[8,2,2,768,256]{4,3,0,2,1:T(8,128)(2,1)}, u32[]{:S(2)}) copy-start(bf16[8,2,2,768,256]{4,3,0,2,1:T(8,128)(2,1)} %all-gather.2.cloned.1.call-done) | copy-start | bytes 37748740
  149.7 5.3 %copy-start.10 = (bf16[2,128,2048]{2,1,0:T(8,128)(2,1)S(1)}, bf16[2,128,2048]{2,1,0:T(8,128)(2,1)}, u32[]{:S(2)}) copy-start(bf16[2,128,2048]{2,1,0:T(8,128)(2,1)} %param.13) | copy-start | bytes 3145732
  156.9 0.7 copy-start.8
  157.0 5.2 %copy-start.5 = (bf16[2,768,128]{2,1,0:T(8,128)(2,1)}, bf16[2,768,128]{2,1,0:T(8,128)(2,1)S(1)}, u32[]{:S(2)}) copy-start(bf16[2,768,128]{2,1,0:T(8,128)(2,1)S(1)} %get-tuple-element.31) | copy-start | bytes 1179652
  157.0 7.0 %copy-start.7 = (bf16[2,768,128]{2,1,0:T(8,128)(2,1)}, bf16[2,768,128]{2,1,0:T(8,128)(2,1)S(1)}, u32[]{:S(2)}) copy-start(bf16[2,768,128]{2,1,0:T(8,128)(2,1)S(1)} %get-tuple-element.30) | copy-start | bytes 1179652
  162.1 93.2 %reduce-scatter.5.cloned.1.call-start = ((), (), s32[]{:S(2)}) async-start(), calls=%async_computation.7 | async-start | bytes 7077888 | tf_op jit(solution)/shard_map/reduce_scatter | solution.py:79
  168.4 52.3 %copy-start.14 = (bf16[128,256]{1,0:T(8,128)(2,1)S(1)}, bf16[128,256]{1,0:T(8,128)(2,1)}, u32[]{:S(2)}) copy-start(bf16[128,256]{1,0:T(8,128)(2,1)} %param.8) | copy-start | bytes 196612
  210.5 47.7 %all-to-all-start.1 = ((bf16[2,768,256]{2,0,1:T(2,128)(2,1)}), bf16[2,768,256]{2,0,1:T(2,128)(2,1)S(1)}, u32[]{:S(2)}, u32[]{:S(2)}) async-start(bf16[2,768,256]{2,0,1:T(2,128)(2,1)} %copy.71), calls=%async_computation.2 | async-start | bytes 1572864 | tf_op jit(solution)/shard_map/all_to_all | solution.py:82
  258.2 17.4 %copy-start.3 = (bf16[2,768,256]{2,0,1:T(2,128)(2,1)}, bf16[2,768,256]{2,0,1:T(2,128)(2,1)S(1)}, u32[]{:S(2)}) copy-start(bf16[2,768,256]{2,0,1:T(2,128)(2,1)S(1)} %all-to-all-done.1) | copy-start | bytes 2359300
  258.2 61.5 %all-to-all-start.2 = ((bf16[2,768,256]{2,0,1:T(2,128)(2,1)}), bf16[2,768,256]{2,0,1:T(2,128)(2,1)}, u32[]{:S(2)}, u32[]{:S(2)}) async-start(bf16[2,768,256]{2,0,1:T(2,128)(2,1)} %copy.74), calls=%async_computation.4 | async-start | bytes 1572864 | tf_op jit(solution)/shard_map/all_to_all | solution.py:83
  275.6 6.7 %copy-start.6 = (bf16[2,768,128]{2,1,0:T(8,128)(2,1)S(1)}, bf16[2,768,128]{2,1,0:T(8,128)(2,1)}, u32[]{:S(2)}) copy-start(bf16[2,768,128]{2,1,0:T(8,128)(2,1)} %copy-done.5) | copy-start | bytes 1179652
  282.3 6.8 %copy-start.4 = (bf16[2,768,256]{2,0,1:T(2,128)(2,1)S(1)}, bf16[2,768,256]{2,0,1:T(2,128)(2,1)}, u32[]{:S(2)}) copy-start(bf16[2,768,256]{2,0,1:T(2,128)(2,1)} %copy-done.3) | copy-start | bytes 2359300
  282.3 10.8 %copy-start.13 = (f32[128,256]{1,0:T(8,128)S(1)}, f32[128,256]{1,0:T(8,128)}, u32[]{:S(2)}) copy-start(f32[128,256]{1,0:T(8,128)} %convert_element_type.91) | copy-start | bytes 393220
  289.1 32.0 %copy-start.12 = (pred[1536,128]{1,0:T(8,128)(4,1)S(1)}, pred[1536,128]{1,0:T(8,128)(4,1)}, u32[]{:S(2)}) copy-start(pred[1536,128]{1,0:T(8,128)(4,1)} %copy-done.11) | copy-start | bytes 589828
  289.1 33.0 %copy-start.1 = (bf16[2,2048,128]{2,1,0:T(8,128)(2,1)S(1)}, bf16[2,2048,128]{2,1,0:T(8,128)(2,1)}, u32[]{:S(2)}) copy-start(bf16[2,2048,128]{2,1,0:T(8,128)(2,1)} %param.11) | copy-start | bytes 3145732
Sparse Core Ops, SparseCore 0:
  78.2 66.7 all-gather.1
  162.2 45.4 reduce-scatter.2
  210.3 44.9 reduce-scatter.4
where the time goes:
time: 329 us
  waiting for transfers between devices  140 us (43%)
  blocking collectives  75.4 us (23%)
  matrix products  46.6 us (14%)
  starting transfers between devices  20.5 us (6%)
  local copies, waits for them, and re-layouts  16.7 us (5%)
  other arithmetic  15.5 us (5%)
  between operations  14.1 us (4%)
    all_gather x1, waiting for transfers between devices, local(): gathered = lax.all_gather(routed, 'et', axis=0)  66.7 us
    all_to_all x1, blocking collectives, local(): lax.all_to_all(routed, 'dp', split_axis=1, concat_axis=2, tiled=True)  50.7 us
    reduce_scatter x1, waiting for transfers between devices, local(): lax.psum_scatter(out_part.astype(jnp.bfloat16), 'et', scatter_dimension=2...  39.3 us
    reduce_scatter x1, waiting for transfers between devices, local(): lax.psum_scatter(in_part.astype(jnp.bfloat16), 'et', scatter_dimension=2,...  33.8 us
    psum x1, blocking collectives, local(): grad_gates = lax.psum(gate_part, 'et')  24.7 us
    all_to_all x1, starting transfers between devices, local(): lax.all_to_all(out_sum, 'dp', split_axis=1, concat_axis=0, tiled=True)  10.1 us
    all_to_all x1, starting transfers between devices, local(): lax.all_to_all(in_sum, 'dp', split_axis=1, concat_axis=0, tiled=True)  10.1 us
    reduce_sum x1, other arithmetic, local(): jnp.sum(jnp.where(match, route_gates.T[None, :, :].astype(jnp.float32), 0...  8.15 us
  transfers between devices with their start and end apart: 5, of which 3 were waited for; matrix products, arithmetic and copies ran while one was open for 12% of the time, Pallas kernels for 0%

commit v1 on v0

--- a/solution.py
+++ b/solution.py
@@ -94,7 +94,7 @@
         back_out[slot_index.reshape(-1)].reshape(tok_rows, per_token, width).astype(jnp.float32)
     )
     gate_part = jnp.sum(cotangent.astype(jnp.float32)[:, None, :] * out_rows, axis=2)
-    grad_gates = lax.psum(gate_part, "et")
+    grad_gates = jnp.sum(lax.all_gather(gate_part, "et"), axis=0)
     return (mixed, grad_tokens, grad_gates, grad_gate_w, grad_up_w, grad_down)
 
 

time: 329 us -> 315 us (0.957)
  blocking collectives: 75.4 us -> 63.8 us
  waiting for transfers between devices: 140 us -> 132 us
    psum x1 -> x0, blocking collectives: 24.7 us -> none  [local(): grad_gates = lax.psum(gate_part, 'et')]
    all_gather x0 -> x1, blocking collectives: none -> 13.1 us  [local(): grad_gates = jnp.sum(lax.all_gather(gate_part, 'et'), axis=0)]
    reduce_scatter x1, waiting for transfers between devices: 33.8 us -> 26.4 us  [local(): lax.psum_scatter(in_part.astype(jnp.bfloat16), 'et', scatter_dimension=2,...]
  transfers between devices with their start and end apart: 5 -> 5, of which waited for: 3 -> 3; matrix products, arithmetic and copies ran while one was open for 12% -> 14% of each run, Pallas kernels for 0% -> 0%
where the time goes in v1:
time: 315 us; the launch traced here: 313 us
  waiting for transfers between devices  132 us (42%)
  blocking collectives  63.8 us (20%)
  matrix products  47.5 us (15%)
  starting transfers between devices  20.5 us (7%)
  other arithmetic  17.8 us (6%)
  local copies, waits for them, and re-layouts  16.9 us (5%)
  between operations  14 us (4%)
    all_gather x1, waiting for transfers between devices, local(): gathered = lax.all_gather(routed, 'et', axis=0)  66.7 us
    all_to_all x1, blocking collectives, local(): lax.all_to_all(routed, 'dp', split_axis=1, concat_axis=2, tiled=True)  50.7 us
    reduce_scatter x1, waiting for transfers between devices, local(): lax.psum_scatter(out_part.astype(jnp.bfloat16), 'et', scatter_dimension=2...  39.3 us
    reduce_scatter x1, waiting for transfers between devices, local(): lax.psum_scatter(in_part.astype(jnp.bfloat16), 'et', scatter_dimension=2,...  26.4 us
    all_gather x1, blocking collectives, local(): grad_gates = jnp.sum(lax.all_gather(gate_part, 'et'), axis=0)  13.1 us
    all_to_all x1, starting transfers between devices, local(): lax.all_to_all(out_sum, 'dp', split_axis=1, concat_axis=0, tiled=True)  10.2 us
    all_to_all x1, starting transfers between devices, local(): lax.all_to_all(in_sum, 'dp', split_axis=1, concat_axis=0, tiled=True)  10 us
    reduce_sum x1, other arithmetic, local(): jnp.sum(jnp.where(match, route_gates.T[None, :, :].astype(jnp.float32), 0...  8.15 us
  transfers between devices with their start and end apart: 5, of which 3 were waited for; matrix products, arithmetic and copies ran while one was open for 14% of the time, Pallas kernels for 0%

profile of v1, /device:TPU:2, one launch (start us, length us, event | category | flops | bytes accessed | tf_op | source)
XLA Modules:
  0.0 312.9 jit_solution(4791672245889796773)
XLA Ops:
  9.6 5.6 %fusion = pred[1536,128]{1,0:T(8,128)(4,1)S(1)} fusion(s32[8,128]{1,0:T(8,128)S(1)} %copy.99), kind=kLoop, calls=%fused_computation.6 | loop fusion | flops 2949120 | bytes 200704 | tf_op jit(solution)/shard_map/reduce_or | solution.py:33
  15.2 8.1 %select_reduce_fusion = bf16[1536,128]{1,0:T(8,128)(2,1)S(1)} fusion(f32[8,128]{1,0:T(8,128)S(1)} %convert_bitcast_fusion, s32[8,128]{1,0:T(8,128)S(1)} %copy.99), kind=kLoop, calls=%fused_computation.4 | loop fusion | flops 4521984 | bytes 401408 | tf_op jit(solution)/shard_map/reduce_sum | solution.py:34
  26.1 50.7 %all_to_all.45 = bf16[2,64,24,256]{3,2,0,1:T(8,128)(2,1)S(1)} all-to-all(bf16[2,64,24,256]{3,2,0,1:T(8,128)(2,1)S(1)} %pad_maximum_fusion), channel_id=1, replica_groups=mesh['dp'=32,'et'=8] {'dp'}, dimensions={1} | all-to-all | bytes 3145728 | tf_op jit(solution)/shard_map/all_to_all | solution.py:42
  78.3 66.7 %all-gather.3.cloned.1.call-done = bf16[8,2,2,768,256]{4,3,0,2,1:T(8,128)(2,1)} async-done(((bf16[1,2,2,768,256]{4,3,0,2,1:T(8,128)(2,1)}), bf16[8,2,2,768,256]{4,3,0,2,1:T(8,128)(2,1)}) %all-gather.3.cloned.1.call-update) | async-done | bytes 12582928 | tf_op jit(solution)/shard_map/all_gather | solution.py:43
  144.9 4.7 %fusion.9 = f32[2,768,128]{2,1,0:T(8,128)S(1)} fusion(bf16[2,8,256,128]{3,2,1,0:T(8,128)(2,1)S(1)} %bitcast.110, bf16[8,2,2,768,256]{4,3,0,2,1:T(8,128)(2,1)} %all-gather.3.cloned.1.call-done), kind=kOutput, calls=%fused_computation.20 | convolution fusion | flops 805306368 | bytes 8126464 | tf_op jit(solution)/shard_map/jesd,ejdf->esf/dot_general | solution.py:50
  149.7 5.2 %fusion.8 = f32[2,768,128]{2,1,0:T(8,128)S(1)} fusion(bf16[2,8,256,128]{3,2,1,0:T(8,128)(2,1)S(1)} %bitcast.98, bf16[8,2,2,768,256]{4,3,0,2,1:T(8,128)(2,1)} %all-gather.3.cloned.1.call-done), kind=kOutput, calls=%fused_computation.19 | convolution fusion | flops 805306368 | bytes 8126464 | tf_op jit(solution)/shard_map/jesd,ejdf->esf/dot_general | solution.py:49
  154.9 2.0 multiply_convert_fusion
  157.7 4.4 %convolution_convert_fusion = bf16[2,768,2048]{2,1,0:T(8,128)(2,1)} fusion(bf16[2,768,128]{2,1,0:T(8,128)(2,1)S(1)} %get-tuple-element.44, bf16[2,128,2048]{2,1,0:T(8,128)(2,1)S(1)} %copy-done.9), kind=kOutput, calls=%fused_computation.9 | convolution fusion | flops 808452096 | bytes 7733248 | tf_op jit(solution)/shard_map/esf,efd->esd/dot_general | solution.py:54
  162.2 1.8 fusion.24
  164.0 4.4 %add_convert_fusion = bf16[2,768,2048]{2,1,0:T(8,128)(2,1)} fusion(f32[2,768,2048]{2,1,0:T(8,128)S(1)} %fusion.24, bf16[2,768,128]{2,1,0:T(8,128)(2,1)S(1)} %get-tuple-element.42, bf16[2,2048,128]{2,1,0:T(8,128)(2,1)S(1)} %copy-done.8), kind=kOutput, calls=%fused_computation.1 | convolution fusion | flops 811597824 | bytes 20316160 | tf_op jit(solution)/shard_map/esf,edf->esd/dot_general | solution.py:74
  168.4 39.3 %reduce-scatter.3.cloned.1.call-done = bf16[2,768,256]{2,1,0:T(8,128)(2,1)} async-done(((bf16[2,768,2048]{2,1,0:T(8,128)(2,1)}), bf16[2,768,256]{2,1,0:T(8,128)(2,1)}) %reduce-scatter.3.cloned.1.call-update) | async-done | bytes 786448 | tf_op jit(solution)/shard_map/reduce_scatter | solution.py:78
  207.7 2.8 copy.103
  210.5 10.2 %all-to-all-start.1 = ((bf16[2,768,256]{2,0,1:T(2,128)(2,1)}), bf16[2,768,256]{2,0,1:T(2,128)(2,1)S(1)}, u32[]{:S(2)}, u32[]{:S(2)}) async-start(bf16[2,768,256]{2,0,1:T(2,128)(2,1)} %copy.103), calls=%async_computation.2 | async-start | bytes 1572864 | tf_op jit(solution)/shard_map/all_to_all | solution.py:82
  221.5 5.6 %fusion.1 = f32[2,128,8,256]{1,3,2,0:T(8,128)S(1)} fusion(bf16[8,2,2,768,256]{4,3,0,2,1:T(8,128)(2,1)} %all-gather.3.cloned.1.call-done, bf16[2,768,128]{2,1,0:T(8,128)(2,1)} %copy-done.7), kind=kOutput, calls=%fused_computation.7 | convolution fusion | flops 805306368 | bytes 8781824 | tf_op jit(solution)/shard_map/esf,jesd->efjd/dot_general | solution.py:62
  227.1 1.8 copy.114
  228.9 26.4 %reduce-scatter.5.cloned.1.call-done = bf16[2,768,256]{2,1,0:T(8,128)(2,1)} async-done(((bf16[2,768,2048]{2,1,0:T(8,128)(2,1)}), bf16[2,768,256]{2,1,0:T(8,128)(2,1)}) %reduce-scatter.5.cloned.1.call-update) | async-done | bytes 786448 | tf_op jit(solution)/shard_map/reduce_scatter | solution.py:79
  255.3 2.9 copy.106
  258.2 10.0 %all-to-all-start.2 = ((bf16[2,768,256]{2,0,1:T(2,128)(2,1)}), bf16[2,768,256]{2,0,1:T(2,128)(2,1)S(1)}, u32[]{:S(2)}, u32[]{:S(2)}) async-start(bf16[2,768,256]{2,0,1:T(2,128)(2,1)} %copy.106), calls=%async_computation.4 | async-start | bytes 1572864 | tf_op jit(solution)/shard_map/all_to_all | solution.py:83
  268.3 6.7 %fusion.4 = f32[2,8,256,128]{3,2,1,0:T(8,128)} fusion(bf16[8,2,2,768,256]{4,3,0,2,1:T(8,128)(2,1)} %all-gather.3.cloned.1.call-done, bf16[2,768,128]{2,1,0:T(8,128)(2,1)} %copy-done.6), kind=kOutput, calls=%fused_computation.12 | convolution fusion | flops 805306368 | bytes 8781824 | tf_op jit(solution)/shard_map/jesd,esf->ejdf/dot_general | solution.py:68
  274.9 6.7 %fusion.5 = f32[2,8,256,128]{3,2,1,0:T(8,128)} fusion(bf16[8,2,2,768,256]{4,3,0,2,1:T(8,128)(2,1)} %all-gather.3.cloned.1.call-done, bf16[2,768,128]{2,1,0:T(8,128)(2,1)S(1)} %copy-done.5), kind=kOutput, calls=%fused_computation.13 | convolution fusion | flops 805306368 | bytes 8781824 | tf_op jit(solution)/shard_map/jesd,esf->ejdf/dot_general | solution.py:65
  282.9 3.9 %gather_fusion = bf16[1024,256]{1,0:T(8,128)(2,1)S(1)} fusion(bf16[1536,256]{1,0:T(8,128)(2,1)S(1)} %bitcast.99, s32[1024]{0:T(1024)S(1)} %broadcast_clamp_fusion), kind=kCustom, calls=%fused_computation | custom fusion | bytes 1052672 | tf_op jit(solution)/shard_map/gather | solution.py:94
  288.0 13.1 %all-gather = f32[1024,8]{1,0:T(8,128)S(1)} all-gather(f32[128,8]{1,0:T(8,128)S(1)} %fusion.15), channel_id=2, replica_groups=mesh['dp'=32,'et'=8] {'et'}, dimensions={0}, use_global_device_ids=true | all-gather | bytes 36864 | tf_op jit(solution)/shard_map/all_gather | solution.py:97
  301.9 1.4 bitcast_reduce_fusion
  304.4 2.0 convolution_convert_fusion.4
  (54 shorter events, 12.5 us)
Async XLA Ops:
  7.2 142.5 %copy-start = (bf16[2,2048,128]{2,1,0:T(8,128)(2,1)S(1)}, bf16[2,2048,128]{2,1,0:T(8,128)(2,1)}, u32[]{:S(2)}) copy-start(bf16[2,2048,128]{2,1,0:T(8,128)(2,1)} %param.11) | copy-start | bytes 3145732
  7.2 137.8 %all-gather.3.cloned.1.call-start = ((), (), s32[]{:S(2)}) async-start(), calls=%async_computation.5 | async-start | bytes 14155776 | tf_op jit(solution)/shard_map/all_gather | solution.py:43
  15.2 10.7 %copy-start.10 = (pred[1536,128]{1,0:T(8,128)(4,1)}, pred[1536,128]{1,0:T(8,128)(4,1)S(1)}, u32[]{:S(2)}) copy-start(pred[1536,128]{1,0:T(8,128)(4,1)S(1)} %fusion) | copy-start | bytes 589828
  24.6 120.4 %copy-start.8 = (bf16[2,2048,128]{2,1,0:T(8,128)(2,1)S(1)}, bf16[2,2048,128]{2,1,0:T(8,128)(2,1)}, u32[]{:S(2)}) copy-start(bf16[2,2048,128]{2,1,0:T(8,128)(2,1)} %param.12) | copy-start | bytes 3145732
  78.0 129.7 %reduce-scatter.3.cloned.1.call-start = ((), (), s32[]{:S(2)}) async-start(), calls=%async_computation.6 | async-start | bytes 7077888 | tf_op jit(solution)/shard_map/reduce_scatter | solution.py:78
  144.9 10.0 %copy-start.2 = (bf16[8,2,2,768,256]{4,3,0,2,1:T(8,128)(2,1)S(1)}, bf16[8,2,2,768,256]{4,3,0,2,1:T(8,128)(2,1)}, u32[]{:S(2)}) copy-start(bf16[8,2,2,768,256]{4,3,0,2,1:T(8,128)(2,1)} %all-gather.3.cloned.1.call-done) | copy-start | bytes 37748740
  149.7 5.3 %copy-start.9 = (bf16[2,128,2048]{2,1,0:T(8,128)(2,1)S(1)}, bf16[2,128,2048]{2,1,0:T(8,128)(2,1)}, u32[]{:S(2)}) copy-start(bf16[2,128,2048]{2,1,0:T(8,128)(2,1)} %param.13) | copy-start | bytes 3145732
  156.9 0.7 copy-start.7
  157.0 5.2 %copy-start.4 = (bf16[2,768,128]{2,1,0:T(8,128)(2,1)}, bf16[2,768,128]{2,1,0:T(8,128)(2,1)S(1)}, u32[]{:S(2)}) copy-start(bf16[2,768,128]{2,1,0:T(8,128)(2,1)S(1)} %get-tuple-element.43) | copy-start | bytes 1179652
  157.0 7.0 %copy-start.6 = (bf16[2,768,128]{2,1,0:T(8,128)(2,1)}, bf16[2,768,128]{2,1,0:T(8,128)(2,1)S(1)}, u32[]{:S(2)}) copy-start(bf16[2,768,128]{2,1,0:T(8,128)(2,1)S(1)} %get-tuple-element.42) | copy-start | bytes 1179652
  162.1 93.2 %reduce-scatter.5.cloned.1.call-start = ((), (), s32[]{:S(2)}) async-start(), calls=%async_computation.7 | async-start | bytes 7077888 | tf_op jit(solution)/shard_map/reduce_scatter | solution.py:79
  168.4 52.3 %copy-start.11 = (bf16[128,256]{1,0:T(8,128)(2,1)S(1)}, bf16[128,256]{1,0:T(8,128)(2,1)}, u32[]{:S(2)}) copy-start(bf16[128,256]{1,0:T(8,128)(2,1)} %param.8) | copy-start | bytes 196612
  210.5 47.7 %all-to-all-start.1 = ((bf16[2,768,256]{2,0,1:T(2,128)(2,1)}), bf16[2,768,256]{2,0,1:T(2,128)(2,1)S(1)}, u32[]{:S(2)}, u32[]{:S(2)}) async-start(bf16[2,768,256]{2,0,1:T(2,128)(2,1)} %copy.103), calls=%async_computation.2 | async-start | bytes 1572864 | tf_op jit(solution)/shard_map/all_to_all | solution.py:82
  228.9 46.0 %copy-start.5 = (bf16[2,768,128]{2,1,0:T(8,128)(2,1)S(1)}, bf16[2,768,128]{2,1,0:T(8,128)(2,1)}, u32[]{:S(2)}) copy-start(bf16[2,768,128]{2,1,0:T(8,128)(2,1)} %copy-done.4) | copy-start | bytes 1179652
  258.2 23.4 %copy-start.3 = (bf16[2,768,256]{2,0,1:T(2,128)(2,1)}, bf16[2,768,256]{2,0,1:T(2,128)(2,1)S(1)}, u32[]{:S(2)}) copy-start(bf16[2,768,256]{2,0,1:T(2,128)(2,1)S(1)} %all-to-all-done.1) | copy-start | bytes 2359300
  258.2 46.0 %all-to-all-start.2 = ((bf16[2,768,256]{2,0,1:T(2,128)(2,1)}), bf16[2,768,256]{2,0,1:T(2,128)(2,1)S(1)}, u32[]{:S(2)}, u32[]{:S(2)}) async-start(bf16[2,768,256]{2,0,1:T(2,128)(2,1)} %copy.106), calls=%async_computation.4 | async-start | bytes 1572864 | tf_op jit(solution)/shard_map/all_to_all | solution.py:83
  281.6 24.8 %copy-start.1 = (bf16[2,2048,128]{2,1,0:T(8,128)(2,1)S(1)}, bf16[2,2048,128]{2,1,0:T(8,128)(2,1)}, u32[]{:S(2)}) copy-start(bf16[2,2048,128]{2,1,0:T(8,128)(2,1)} %param.11) | copy-start | bytes 3145732
Sparse Core Ops, SparseCore 0:
  78.2 66.7 all-gather.2
  162.2 45.4 reduce-scatter.2
  210.3 45.0 reduce-scatter.4
